TPU v7x, 256 devices: a whole 4x4x8 slice. The times are simulated.
256 devices in a mesh: dp: 32 (over x, z), tensor: 8 (over y, core).
Axes of the slice: x: 4, y: 4, z: 8, core: 2. Of those that a mesh axis runs over, the one named last changes fastest.
Arguments:
- counts: int32 [32], replicated, may hold values from 1 to 32, 512 in all
- keys: bfloat16 [1024, 28672], P('dp'), may hold values from -6 to 6
- inverse_cov: bfloat16 [28672, 28672], P('tensor', 'dp'), as said below
- hidden: bfloat16 [1024, 8192], P('dp', 'tensor'), may hold values from -6 to 6
- targets: bfloat16 [1024, 8192], P('dp', 'tensor'), may hold values from -48 to 48
- down_weight: bfloat16 [8192, 28672], P('tensor', 'dp'), may hold values from -0.03125 to 0.03125
Outputs:
- new_weight: bfloat16 [8192, 28672], P('tensor', 'dp')
- next_resid: bfloat16 [1024, 8192], P('dp', 'tensor')
Inputs may be any that keep to these rules, and one draw needn't show every extreme that they name: Group g has counts[g] live edits in its first counts[g] slots; the counts sum to 512; some group holds 32. `inverse_cov`: symmetric positive definite.
All inputs are finite; a program needn't handle non-finite values.
Results may differ from a plain program's by a relative error of at most 0.01.
The roundings to bfloat16 on the way count: a program that leaves them out, or rounds other values in their place, can miss the bound.
Values may be sent and summed in bfloat16 or wider, within the bound.
No kernel may reach another device: no remote copies, remote signals or barrier semaphores. Data moves between devices by JAX's collectives and lax.ppermute only.
A program may use at most 128 MiB of HBM per device.

v0:
```python
import jax
import jax.numpy as jnp
from jax import lax
from jax.sharding import PartitionSpec as P

LAYERS_LEFT = 3


def cholesky_solve(system, right_side):
    factor = jnp.linalg.cholesky(system)
    middle = lax.linalg.triangular_solve(factor, right_side, left_side=True, lower=True)
    return lax.linalg.triangular_solve(factor, middle, left_side=True, lower=True, transpose_a=True)


def rows_product(left, right):
    return lax.dot_general(
        left, right, (((1,), (1,)), ((), ())), preferred_element_type=jnp.float32
    )


def pick(select, values):
    return jnp.dot(select, values, preferred_element_type=jnp.float32).astype(values.dtype)


def per_device(counts, keys, inverse_cov, hidden, targets, down_weight):
    slot_count = keys.shape[0]
    group_size = lax.axis_size("dp")
    group_index = lax.axis_index("dp")
    tensor_index = lax.axis_index("tensor")
    width_part = inverse_cov.shape[0]
    row_total = slot_count * group_size
    live_total = row_total // 2
    ends = jnp.cumsum(counts)
    starts = ends - counts
    compact = jnp.arange(live_total, dtype=jnp.int32)
    owner = jnp.minimum(jnp.sum(compact[:, None] >= ends[None, :], axis=1), group_size - 1)
    row_of = owner * slot_count + compact - starts[owner]
    select = (row_of[:, None] == jnp.arange(row_total, dtype=jnp.int32)[None, :]).astype(
        jnp.bfloat16
    )
    slots = jnp.arange(slot_count, dtype=jnp.int32)
    live_vec = slots < counts[group_index]
    live_slot = live_vec[:, None]
    own_compact = jnp.where(live_vec, starts[group_index] + slots, 0)
    masked_keys = jnp.where(live_slot, keys, jnp.zeros_like(keys))
    column_part = lax.dynamic_slice_in_dim(masked_keys, tensor_index * width_part, width_part, 1)
    columns = lax.all_to_all(masked_keys, "dp", split_axis=1, concat_axis=0, tiled=True)
    gathered = lax.all_gather(column_part, "dp", axis=0, tiled=True)
    keys_c = pick(select, gathered)
    columns_c = pick(select, columns)
    partial_q = jnp.dot(keys_c, inverse_cov, preferred_element_type=jnp.float32)
    precond_c = lax.psum(partial_q, "tensor").astype(jnp.bfloat16)
    gram_c = lax.psum(rows_product(precond_c, columns_c), "dp")
    base_partial = rows_product(columns, down_weight)
    gram_c, base_partial = lax.optimization_barrier((gram_c, base_partial))
    base = lax.psum_scatter(base_partial, "dp", scatter_dimension=0, tiled=True)
    system = gram_c + jnp.eye(live_total, dtype=jnp.float32)
    change = (targets.astype(jnp.float32) - hidden.astype(jnp.float32)) / LAYERS_LEFT
    resid_local = jnp.where(live_slot, change, jnp.zeros_like(change)).astype(jnp.bfloat16)
    resid_all = lax.all_gather(resid_local, "dp", axis=0, tiled=True)
    resid_c = pick(select, resid_all)
    solved_c = cholesky_solve(system, resid_c.astype(jnp.float32)).astype(jnp.bfloat16)
    weight_delta = lax.dot_general(
        solved_c, precond_c, (((0,), (0,)), ((), ())), preferred_element_type=jnp.float32
    )
    new_weight = (down_weight.astype(jnp.float32) + weight_delta).astype(jnp.bfloat16)
    gram_own = jnp.where(live_slot, jnp.take(gram_c, own_compact, axis=1).T, 0.0)
    extra = jnp.dot(
        gram_own,
        solved_c.astype(jnp.float32),
        precision=lax.Precision.HIGHEST,
        preferred_element_type=jnp.float32,
    )
    summed = hidden.astype(jnp.float32) + (base + extra)
    next_resid = jnp.where(live_slot, summed, jnp.zeros_like(summed)).astype(jnp.bfloat16)
    return (new_weight, next_resid)


def solution(mesh):
    in_specs = (
        P(),
        P("dp", None),
        P("tensor", "dp"),
        P("dp", "tensor"),
        P("dp", "tensor"),
        P("tensor", "dp"),
    )
    out_specs = (P("tensor", "dp"), P("dp", "tensor"))
    return jax.shard_map(
        per_device, mesh=mesh, in_specs=in_specs, out_specs=out_specs, check_vma=False
    )
```

profile of v0, /device:TPU:8, one launch (start us, length us, event | category | flops | bytes accessed | tf_op | source)
XLA Modules:
  0.0 581.5 jit_solution(14730715012602335396)
XLA Ops:
  12.8 11.4 %all-to-all-start = ((bf16[32,32,896]{2,0,1:T(8,128)(2,1)}), bf16[32,32,896]{2,0,1:T(8,128)(2,1)S(1)}, u32[]{:S(2)}, u32[]{:S(2)}) async-start(bf16[32,32,896]{2,0,1:T(8,128)(2,1)} %bitcast.118), calls=%async_computation | async-start | bytes 3670016 | tf_op jit(solution)/shard_map/all_to_all | solution.py:47
  26.9 4.5 compare_select_fusion.1
  31.6 15.7 %select_subtract_fusion = s32[512]{0:T(512)S(1)} fusion(pred[512]{0:T(512)(128)(4,1)S(1)} %get-tuple-element.38, pred[512]{0:T(512)(128)(4,1)S(1)} %get-tuple-element.37, pred[512]{0:T(512)(128)(4,1)S(1)} %get-tuple-element.36, pred[512]{0:T(512)(128)(4,1)S(1)} %get-tuple-element.35, pred[512]{0:T(512)(128)(4,1)S(1)} %get-tuple-element.34, ...), kind=kLoop, calls=%fused_computation.145 | loop fusion | flops 14848 | bytes 19044 | tf_op jit(solution)/shard_map/sub | solution.py:37
  49.0 69.0 %all-gather.3.cloned.1.call-done = bf16[1024,3584]{1,0:T(8,128)(2,1)} async-done(((bf16[32,3584]{1,0:T(8,128)(2,1)}), bf16[1024,3584]{1,0:T(8,128)(2,1)}) %all-gather.3.cloned.1.call-update) | async-done | bytes 7340048 | tf_op jit(solution)/shard_map/all_gather | solution.py:48
  118.0 14.0 %fusion.35 = f32[512,896]{1,0:T(8,128)} fusion(bf16[3584,896]{1,0:T(8,128)(2,1)} %param.8, bf16[1024,3584]{1,0:T(8,128)(2,1)} %all-gather.3.cloned.1.call-done, s32[512]{0:T(512)S(1)} %select_subtract_fusion), kind=kOutput, calls=%fused_computation.56 | convolution fusion | flops 7048790016 | bytes 15599616 | tf_op jit(solution)/shard_map/dot_general | solution.py:51
  132.0 50.5 %all-reduce.5 = bf16[512,896]{1,0:T(8,128)(2,1)S(1)} all-reduce(f32[512,896]{1,0:T(8,128)} %fusion.35), channel_id=1, replica_groups=mesh['dp'=32,'tensor'=8] {'tensor'}, use_global_device_ids=true, to_apply=%region_2.3 | all-reduce | flops 458752 | bytes 2752512 | tf_op jit(solution)/shard_map/psum | solution.py:52
  182.5 2.8 fusion.36
  187.4 5.8 fusion.89
  193.2 3.1 all-gather.5.cloned.1.call-done
  196.3 4.5 fusion.85
  200.8 146.6 %all-reduce.4.cloned.1.call-done = f32[512,512]{0,1:T(8,128)} async-done(((f32[512,512]{0,1:T(8,128)}), f32[512,512]{0,1:T(8,128)}) %all-reduce.4.cloned.1.call-update) | async-done | bytes 1048592 | tf_op jit(solution)/shard_map/psum | solution.py:53
  350.6 11.7 %cholesky.104 = f32[128,128]{1,0:T(8,128)S(1)} custom-call(f32[128,128]{1,0:T(8,128)S(1)} %cholesky.266), custom_call_target="Cholesky" | custom-call | tf_op jit(solution)/shard_map/jit(cholesky)/cholesky | solution.py:10
  362.4 9.8 %custom-call.32 = f32[1,128,128]{1,2,0:T(8,128)S(1)} custom-call(f32[1,128,128]{2,1,0:T(8,128)S(1)} %get-tuple-element.60), custom_call_target="InvertDiagBlocksLowerTriangular" | custom-call | tf_op jit(solution)/shard_map/jit(cholesky)/cholesky | solution.py:10
  372.9 12.1 %cholesky.217 = f32[128,128]{1,0:T(8,128)S(1)} custom-call(f32[128,128]{1,0:T(8,128)S(1)} %cholesky.270), custom_call_target="Cholesky" | custom-call | tf_op jit(solution)/shard_map/jit(cholesky)/cholesky | solution.py:10
  385.1 9.8 %custom-call.33 = f32[1,128,128]{1,2,0:T(8,128)S(1)} custom-call(f32[1,128,128]{2,1,0:T(8,128)S(1)} %get-tuple-element.57), custom_call_target="InvertDiagBlocksLowerTriangular" | custom-call | tf_op jit(solution)/shard_map/jit(cholesky)/cholesky | solution.py:10
  395.5 11.7 %cholesky.238 = f32[128,128]{1,0:T(8,128)S(1)} custom-call(f32[128,128]{1,0:T(8,128)S(1)} %cholesky.275), custom_call_target="Cholesky" | custom-call | tf_op jit(solution)/shard_map/jit(cholesky)/cholesky | solution.py:10
  407.3 9.8 %custom-call.34 = f32[1,128,128]{1,2,0:T(8,128)S(1)} custom-call(f32[1,128,128]{2,1,0:T(8,128)S(1)} %get-tuple-element.54), custom_call_target="InvertDiagBlocksLowerTriangular" | custom-call | tf_op jit(solution)/shard_map/jit(cholesky)/cholesky | solution.py:10
  417.7 11.9 %cholesky.255 = f32[128,128]{1,0:T(8,128)S(1)} custom-call(f32[128,128]{1,0:T(8,128)S(1)} %convolution_subtract_fusion.6), custom_call_target="Cholesky" | custom-call | tf_op jit(solution)/shard_map/jit(cholesky)/cholesky | solution.py:10
  434.7 10.0 %while.1 = (s32[]{:T(128)}, f32[512,512]{1,0:T(8,128)S(1)}, s32[4,2]{0,1:T(2,128)S(1)}, f32[4,128,128]{2,1,0:T(8,128)}, s32[]{:T(128)}) while((s32[]{:T(128)}, f32[512,512]{1,0:T(8,128)S(1)}, s32[4,2]{0,1:T(2,128)S(1)}, f32[4,128,128]{2,1,0:T(8,128)}, s32[]{:T(128)}) %tuple.93), condition=%wide.while_cond, body=%wide.while_body.sunk | while | flops 2 | bytes 132205 | solution.py:12
  440.3 1.9 bitcast_dynamic-update-slice_fusion.2
  444.7 40.1 %custom-call.35 = f32[4,128,128]{1,2,0:T(8,128)S(1)} custom-call(f32[4,128,128]{2,1,0:T(8,128)} %get-tuple-element.13), custom_call_target="InvertDiagBlocksLowerTriangular" | custom-call | tf_op jit(solution)/shard_map/triangular_solve | solution.py:12
  497.3 2.6 add_convert_fusion
  499.9 72.7 %reduce-scatter.2.cloned.1.call-done = f32[32,1024]{1,0:T(8,128)} async-done(((f32[1024,1024]{1,0:T(8,128)}), f32[32,1024]{1,0:T(8,128)}) %reduce-scatter.2.cloned.1.call-update) | async-done | bytes 131088 | tf_op jit(solution)/shard_map/reduce_scatter | solution.py:56
  572.6 2.2 fusion.24
  (95 shorter events, 40.3 us)
Async XLA Ops:
  7.2 110.9 %all-gather.3.cloned.1.call-start = ((), (), s32[]{:S(2)}) async-start(), calls=%async_computation.2 | async-start | bytes 7569408 | tf_op jit(solution)/shard_map/all_gather | solution.py:48
  12.8 11.5 %copy-start.4 = (bf16[32,1024]{1,0:T(8,128)(2,1)S(1)}, bf16[32,1024]{1,0:T(8,128)(2,1)}, u32[]{:S(2)}) copy-start(bf16[32,1024]{1,0:T(8,128)(2,1)} %param.10) | copy-start | bytes 196612
  12.8 11.5 %copy-start.5 = (bf16[32,1024]{1,0:T(8,128)(2,1)S(1)}, bf16[32,1024]{1,0:T(8,128)(2,1)}, u32[]{:S(2)}) copy-start(bf16[32,1024]{1,0:T(8,128)(2,1)} %param.9) | copy-start | bytes 196612
  12.8 12.3 %copy-start.6 = (s32[32]{0:T(128)S(1)}, s32[32]{0:T(128)}, u32[]{:S(2)}) copy-start(s32[32]{0:T(128)} %param.6) | copy-start | bytes 388
  12.8 169.7 %all-to-all-start = ((bf16[32,32,896]{2,0,1:T(8,128)(2,1)}), bf16[32,32,896]{2,0,1:T(8,128)(2,1)S(1)}, u32[]{:S(2)}, u32[]{:S(2)}) async-start(bf16[32,32,896]{2,0,1:T(8,128)(2,1)} %bitcast.118), calls=%async_computation | async-start | bytes 3670016 | tf_op jit(solution)/shard_map/all_to_all | solution.py:47
  24.3 172.0 %all-gather.5.cloned.1.call-start = ((), (), s32[]{:S(2)}) async-start(), calls=%async_computation.4 | async-start | bytes 2162688 | tf_op jit(solution)/shard_map/all_gather | solution.py:60
  25.1 322.4 %all-reduce.4.cloned.1.call-start = ((), (), s32[]{:S(2)}) async-start(), calls=%async_computation.3 | async-start | bytes 2097152 | tf_op jit(solution)/shard_map/psum | solution.py:53
  182.5 2.8 copy-start.2
  185.4 387.2 %reduce-scatter.2.cloned.1.call-start = ((), (), s32[]{:S(2)}) async-start(), calls=%async_computation.5 | async-start | bytes 4325376 | tf_op jit(solution)/shard_map/reduce_scatter | solution.py:56
  349.1 1.2 copy-start
  485.5 3.8 copy-start.1
  495.5 1.7 copy-start.3
  495.5 1.8 copy-start.7
  497.3 75.2 %copy-start.8 = (pred[32]{0:T(512)(128)(4,1)S(1)}, pred[32]{0:T(512)(128)(4,1)}, u32[]{:S(2)}) copy-start(pred[32]{0:T(512)(128)(4,1)} %compare_and_fusion) | copy-start | bytes 100
Sparse Core Ops, SparseCore 0:
  11.5 106.4 all-gather.2
  121.2 75.0 all-gather.4
  199.7 147.6 all-reduce.3
  351.2 221.3 reduce-scatter.1
where the time goes:
time: 589 us; the launch traced here: 582 us
  waiting for transfers between devices  291 us (49%)
  other arithmetic  148 us (25%)
  blocking collectives  50.5 us (9%)
  matrix products  45.4 us (8%)
  local copies, waits for them, and re-layouts  17.8 us (3%)
  between operations  16.9 us (3%)
  starting transfers between devices  11.8 us (2%)
    psum x1, waiting for transfers between devices, per_device(): gram_c = lax.psum(rows_product(precond_c, columns_c), 'dp')  147 us
    another operation x14, other arithmetic, cholesky_solve(): factor = jnp.linalg.cholesky(system)  78.9 us
    reduce_scatter x1, waiting for transfers between devices, per_device(): base = lax.psum_scatter(base_partial, 'dp', scatter_dimension=0, tiled=True)  72.7 us
    all_gather x1, waiting for transfers between devices, per_device(): gathered = lax.all_gather(column_part, 'dp', axis=0, tiled=True)  69 us
    psum x1, blocking collectives, per_device(): precond_c = lax.psum(partial_q, 'tensor').astype(jnp.bfloat16)  50.5 us
    another operation x3, other arithmetic, cholesky_solve(): lax.linalg.triangular_solve(factor, middle, left_side=True, lower=True, t...  40.7 us
    sub x1, other arithmetic, per_device(): row_of = owner * slot_count + compact - starts[owner]  15.7 us
    dot_general x1, matrix products, per_device(): partial_q = jnp.dot(keys_c, inverse_cov, preferred_element_type=jnp.float32)  14 us
  transfers between devices with their start and end apart: 5, of which 4 were waited for; matrix products, arithmetic and copies ran while one was open for 35% of the time, Pallas kernels for 0%

commit v1 on v0

--- a/solution.py
+++ b/solution.py
@@ -2,6 +2,7 @@
 import jax.numpy as jnp
 from jax import lax
 from jax.sharding import PartitionSpec as P
+from jax.lax import all_gather
 
 LAYERS_LEFT = 3
 
@@ -50,7 +51,11 @@
     columns_c = pick(select, columns)
     partial_q = jnp.dot(keys_c, inverse_cov, preferred_element_type=jnp.float32)
     precond_c = lax.psum(partial_q, "tensor").astype(jnp.bfloat16)
-    gram_c = lax.psum(rows_product(precond_c, columns_c), "dp")
+
+    def domain_expand(m):
+        return jnp.sum(all_gather(m, axis_name="dp"), 0)
+
+    gram_c = domain_expand(rows_product(precond_c, columns_c))
     base_partial = rows_product(columns, down_weight)
     gram_c, base_partial = lax.optimization_barrier((gram_c, base_partial))
     base = lax.psum_scatter(base_partial, "dp", scatter_dimension=0, tiled=True)

time: 589 us -> 681 us (1.16)
  waiting for transfers between devices: 291 us -> 372 us
  other arithmetic: 148 us -> 158 us
    all_gather x0 -> x1, waiting for transfers between devices: none -> 228 us  [domain_expand(): return jnp.sum(all_gather(m, axis_name='dp'), 0)]
    psum x1 -> x0, waiting for transfers between devices: 147 us -> none  [per_device(): gram_c = lax.psum(rows_product(precond_c, columns_c), 'dp')]
    reduce_sum x0 -> x1, other arithmetic: none -> 12.4 us  [domain_expand(): return jnp.sum(all_gather(m, axis_name='dp'), 0)]
  transfers between devices with their start and end apart: 5 -> 5, of which waited for: 4 -> 4; matrix products, arithmetic and copies ran while one was open for 35% -> 30% of each run, Pallas kernels for 0% -> 0%
where the time goes in v1:
time: 681 us; the launch traced here: 672 us
  waiting for transfers between devices  372 us (55%)
  other arithmetic  158 us (23%)
  blocking collectives  50.5 us (7%)
  matrix products  45.5 us (7%)
  local copies, waits for them, and re-layouts  17.8 us (3%)
  between operations  17 us (2%)
  starting transfers between devices  11.6 us (2%)
    all_gather x1, waiting for transfers between devices, domain_expand(): return jnp.sum(all_gather(m, axis_name='dp'), 0)  228 us
    another operation x14, other arithmetic, cholesky_solve(): factor = jnp.linalg.cholesky(system)  78.9 us
    all_gather x1, waiting for transfers between devices, per_device(): gathered = lax.all_gather(column_part, 'dp', axis=0, tiled=True)  71.1 us
    reduce_scatter x1, waiting for transfers between devices, per_device(): base = lax.psum_scatter(base_partial, 'dp', scatter_dimension=0, tiled=True)  70.8 us
    psum x1, blocking collectives, per_device(): precond_c = lax.psum(partial_q, 'tensor').astype(jnp.bfloat16)  50.5 us
    another operation x3, other arithmetic, cholesky_solve(): lax.linalg.triangular_solve(factor, middle, left_side=True, lower=True, t...  40.8 us
    sub x1, other arithmetic, per_device(): row_of = owner * slot_count + compact - starts[owner]  15.2 us
    dot_general x1, matrix products, per_device(): partial_q = jnp.dot(keys_c, inverse_cov, preferred_element_type=jnp.float32)  14 us
  transfers between devices with their start and end apart: 5, of which 4 were waited for; matrix products, arithmetic and copies ran while one was open for 30% of the time, Pallas kernels for 0%

profile of v1, /device:TPU:8, one launch (start us, length us, event | category | flops | bytes accessed | tf_op | source)
XLA Modules:
  0.0 672.3 jit_solution(10021037839605141730)
XLA Ops:
  13.0 11.4 %all-to-all-start = ((bf16[32,32,896]{2,0,1:T(8,128)(2,1)}), bf16[32,32,896]{2,0,1:T(8,128)(2,1)S(1)}, u32[]{:S(2)}, u32[]{:S(2)}) async-start(bf16[32,32,896]{2,0,1:T(8,128)(2,1)} %bitcast.120), calls=%async_computation | async-start | bytes 3670016 | tf_op jit(solution)/shard_map/all_to_all | solution.py:48
  27.1 4.2 compare_select_fusion.1
  31.5 15.2 %select_subtract_fusion = s32[512]{0:T(512)S(1)} fusion(pred[512]{0:T(512)(128)(4,1)S(1)} %get-tuple-element.38, pred[512]{0:T(512)(128)(4,1)S(1)} %get-tuple-element.37, pred[512]{0:T(512)(128)(4,1)S(1)} %get-tuple-element.36, pred[512]{0:T(512)(128)(4,1)S(1)} %get-tuple-element.35, pred[512]{0:T(512)(128)(4,1)S(1)} %get-tuple-element.34, ...), kind=kLoop, calls=%fused_computation.145 | loop fusion | flops 14848 | bytes 19044 | tf_op jit(solution)/shard_map/sub | solution.py:38
  46.7 71.1 %all-gather.5.cloned.1.call-done = bf16[1024,3584]{1,0:T(8,128)(2,1)} async-done(((bf16[32,3584]{1,0:T(8,128)(2,1)}), bf16[1024,3584]{1,0:T(8,128)(2,1)}) %all-gather.5.cloned.1.call-update) | async-done | bytes 7340048 | tf_op jit(solution)/shard_map/all_gather | solution.py:49
  117.8 14.0 %fusion.35 = f32[512,896]{1,0:T(8,128)} fusion(bf16[3584,896]{1,0:T(8,128)(2,1)} %param.8, bf16[1024,3584]{1,0:T(8,128)(2,1)} %all-gather.5.cloned.1.call-done, s32[512]{0:T(512)S(1)} %select_subtract_fusion), kind=kOutput, calls=%fused_computation.56 | convolution fusion | flops 7048790016 | bytes 15599616 | tf_op jit(solution)/shard_map/dot_general | solution.py:52
  131.8 50.5 %all-reduce.2 = bf16[512,896]{1,0:T(8,128)(2,1)S(1)} all-reduce(f32[512,896]{1,0:T(8,128)} %fusion.35), channel_id=1, replica_groups=mesh['dp'=32,'tensor'=8] {'tensor'}, use_global_device_ids=true, to_apply=%region_2.3 | all-reduce | flops 458752 | bytes 2752512 | tf_op jit(solution)/shard_map/psum | solution.py:53
  182.3 2.8 fusion.36
  188.6 5.9 fusion.89
  196.1 4.5 fusion.85
  200.6 228.2 %all-gather.9.cloned.1.call-done = f32[16384,512]{1,0:T(8,128)} async-done(((f32[512,512]{1,0:T(8,128)}), f32[16384,512]{1,0:T(8,128)}) %all-gather.9.cloned.1.call-update) | async-done | bytes 33554448 | tf_op jit(solution)/shard_map/all_gather | solution.py:56
  428.8 12.4 %reduce_sum.19 = f32[512,512]{1,0:T(8,128)S(1)} reduce(f32[32,512,512]{2,1,0:T(8,128)} %bitcast.118, f32[]{:T(128)} %constant.183.clone.1), dimensions={0}, to_apply=%region_3.4 | reduce | flops 8126464 | bytes 34603012 | tf_op jit(solution)/shard_map/reduce_sum | solution.py:56
  442.3 11.7 %cholesky.104 = f32[128,128]{1,0:T(8,128)S(1)} custom-call(f32[128,128]{1,0:T(8,128)S(1)} %cholesky.266), custom_call_target="Cholesky" | custom-call | tf_op jit(solution)/shard_map/jit(cholesky)/cholesky | solution.py:11
  454.2 9.8 %custom-call.32 = f32[1,128,128]{1,2,0:T(8,128)S(1)} custom-call(f32[1,128,128]{2,1,0:T(8,128)S(1)} %get-tuple-element.60), custom_call_target="InvertDiagBlocksLowerTriangular" | custom-call | tf_op jit(solution)/shard_map/jit(cholesky)/cholesky | solution.py:11
  464.7 11.7 %cholesky.217 = f32[128,128]{1,0:T(8,128)S(1)} custom-call(f32[128,128]{1,0:T(8,128)S(1)} %cholesky.270), custom_call_target="Cholesky" | custom-call | tf_op jit(solution)/shard_map/jit(cholesky)/cholesky | solution.py:11
  476.4 10.2 %custom-call.33 = f32[1,128,128]{1,2,0:T(8,128)S(1)} custom-call(f32[1,128,128]{2,1,0:T(8,128)S(1)} %get-tuple-element.57), custom_call_target="InvertDiagBlocksLowerTriangular" | custom-call | tf_op jit(solution)/shard_map/jit(cholesky)/cholesky | solution.py:11
  487.3 11.7 %cholesky.238 = f32[128,128]{1,0:T(8,128)S(1)} custom-call(f32[128,128]{1,0:T(8,128)S(1)} %cholesky.275), custom_call_target="Cholesky" | custom-call | tf_op jit(solution)/shard_map/jit(cholesky)/cholesky | solution.py:11
  499.1 9.8 %custom-call.34 = f32[1,128,128]{1,2,0:T(8,128)S(1)} custom-call(f32[1,128,128]{2,1,0:T(8,128)S(1)} %get-tuple-element.54), custom_call_target="InvertDiagBlocksLowerTriangular" | custom-call | tf_op jit(solution)/shard_map/jit(cholesky)/cholesky | solution.py:11
  509.5 11.9 %cholesky.255 = f32[128,128]{1,0:T(8,128)S(1)} custom-call(f32[128,128]{1,0:T(8,128)S(1)} %convolution_subtract_fusion.6), custom_call_target="Cholesky" | custom-call | tf_op jit(solution)/shard_map/jit(cholesky)/cholesky | solution.py:11
  526.7 10.7 %while.1 = (s32[]{:T(128)}, f32[512,512]{1,0:T(8,128)S(1)}, s32[4,2]{0,1:T(2,128)S(1)}, f32[4,128,128]{2,1,0:T(8,128)}, s32[]{:T(128)}) while((s32[]{:T(128)}, f32[512,512]{1,0:T(8,128)S(1)}, s32[4,2]{0,1:T(2,128)S(1)}, f32[4,128,128]{2,1,0:T(8,128)}, s32[]{:T(128)}) %tuple.93), condition=%wide.while_cond, body=%wide.while_body.sunk | while | flops 2 | bytes 132705 | solution.py:13
  530.1 2.0 bitcast_dynamic-update-slice_fusion.2
  537.4 40.1 %custom-call.35 = f32[4,128,128]{1,2,0:T(8,128)S(1)} custom-call(f32[4,128,128]{2,1,0:T(8,128)} %get-tuple-element.13), custom_call_target="InvertDiagBlocksLowerTriangular" | custom-call | tf_op jit(solution)/shard_map/triangular_solve | solution.py:13
  590.0 2.6 add_convert_fusion
  592.6 70.8 %reduce-scatter.2.cloned.1.call-done = f32[32,1024]{1,0:T(8,128)} async-done(((f32[1024,1024]{1,0:T(8,128)}), f32[32,1024]{1,0:T(8,128)}) %reduce-scatter.2.cloned.1.call-update) | async-done | bytes 131088 | tf_op jit(solution)/shard_map/reduce_scatter | solution.py:61
  663.4 2.2 fusion.24
  (95 shorter events, 40.4 us)
Async XLA Ops:
  7.2 110.6 %all-gather.5.cloned.1.call-start = ((), (), s32[]{:S(2)}) async-start(), calls=%async_computation.2 | async-start | bytes 7569408 | tf_op jit(solution)/shard_map/all_gather | solution.py:49
  13.0 11.5 %copy-start.3 = (bf16[32,1024]{1,0:T(8,128)(2,1)S(1)}, bf16[32,1024]{1,0:T(8,128)(2,1)}, u32[]{:S(2)}) copy-start(bf16[32,1024]{1,0:T(8,128)(2,1)} %param.10) | copy-start | bytes 196612
  13.0 11.5 %copy-start.4 = (bf16[32,1024]{1,0:T(8,128)(2,1)S(1)}, bf16[32,1024]{1,0:T(8,128)(2,1)}, u32[]{:S(2)}) copy-start(bf16[32,1024]{1,0:T(8,128)(2,1)} %param.9) | copy-start | bytes 196612
  13.0 12.3 %copy-start.5 = (s32[32]{0:T(128)S(1)}, s32[32]{0:T(128)}, u32[]{:S(2)}) copy-start(s32[32]{0:T(128)} %param.6) | copy-start | bytes 388
  13.0 169.3 %all-to-all-start = ((bf16[32,32,896]{2,0,1:T(8,128)(2,1)}), bf16[32,32,896]{2,0,1:T(8,128)(2,1)S(1)}, u32[]{:S(2)}, u32[]{:S(2)}) async-start(bf16[32,32,896]{2,0,1:T(8,128)(2,1)} %bitcast.120), calls=%async_computation | async-start | bytes 3670016 | tf_op jit(solution)/shard_map/all_to_all | solution.py:48
  24.5 171.6 %all-gather.7.cloned.1.call-start = ((), (), s32[]{:S(2)}) async-start(), calls=%async_computation.3 | async-start | bytes 2162688 | tf_op jit(solution)/shard_map/all_gather | solution.py:65
  25.3 403.5 %all-gather.9.cloned.1.call-start = ((), (), s32[]{:S(2)}) async-start(), calls=%async_computation.5 | async-start | bytes 34603008 | tf_op jit(solution)/shard_map/all_gather | solution.py:56
  182.3 2.9 copy-start.1
  185.2 478.2 %reduce-scatter.2.cloned.1.call-start = ((), (), s32[]{:S(2)}) async-start(), calls=%async_computation.4 | async-start | bytes 4325376 | tf_op jit(solution)/shard_map/reduce_scatter | solution.py:61
  578.2 3.8 copy-start
  588.2 1.7 copy-start.2
  588.2 1.8 copy-start.6
  590.0 73.3 %copy-start.7 = (pred[32]{0:T(512)(128)(4,1)S(1)}, pred[32]{0:T(512)(128)(4,1)}, u32[]{:S(2)}) copy-start(pred[32]{0:T(512)(128)(4,1)} %compare_and_fusion) | copy-start | bytes 100
Sparse Core Ops, SparseCore 0:
  11.6 106.1 all-gather.4
  121.0 75.0 all-gather.6
  198.7 230.0 all-gather.8
  442.2 221.1 reduce-scatter.1
